TPU v7x, 256 devices: a whole 4x4x8 slice. The times are simulated.
256 devices in a mesh: ctx: 16 (over x_lo, z), fsdp: 4 (over y), head: 4 (over x_hi, core).
Axes of the slice: x: 4 (x_hi: 2, x_lo: 2; x = x_hi * 2 + x_lo), y: 4, z: 8, core: 2. Of those that a mesh axis runs over, the one named last changes fastest.
Arguments:
- queries: bfloat16 [4, 8192, 2048], P('fsdp', 'ctx', 'head'), may hold values from -6 to 6
- keys: bfloat16 [4, 8192, 2048], P('fsdp', 'ctx', 'head'), may hold values from -6 to 6
- values: bfloat16 [4, 8192, 2048], P('fsdp', 'ctx', 'head'), may hold values from -6 to 6
- gate_pre: bfloat16 [4, 8192, 2048], P('fsdp', 'ctx', 'head'), may hold values from -6 to 6
- log_decay: float32 [4, 8192, 16], P('fsdp', 'ctx', 'head'), may hold values from -2 to 0, as said below
- out_grad: bfloat16 [4, 8192, 4096], P('fsdp', 'ctx', 'head'), may hold values from -6 to 6
- out_weight: float32 [4096, 2048], P(('ctx', 'fsdp'), 'head'), may hold values from -0.125 to 0.125
- moment_one: float32 [4096, 2048], P(('ctx', 'fsdp'), 'head'), may hold values from -2 to 2
- moment_two: float32 [4096, 2048], P(('ctx', 'fsdp'), 'head'), may hold values from 0.05 to 1
- group_ids: int32 [128], P(('ctx', 'fsdp')), may hold values from 0 to 2
- step_count: int32 [1], replicated, may hold values from 1 to 40
Outputs:
- query_grad: bfloat16 [4, 8192, 2048], P('fsdp', 'ctx', 'head')
- key_grad: bfloat16 [4, 8192, 2048], P('fsdp', 'ctx', 'head')
- value_grad: bfloat16 [4, 8192, 2048], P('fsdp', 'ctx', 'head')
- new_moment_one: float32 [4096, 2048], P(('ctx', 'fsdp'), 'head')
- new_moment_two: float32 [4096, 2048], P(('ctx', 'fsdp'), 'head')
- weight_step: float32 [4096, 2048], P(('ctx', 'fsdp'), 'head')
Inputs may be any that keep to these rules, and one draw needn't show every extreme that they name: `log_decay`: Log-decays per token and head, never positive. `group_ids`: 0 for a frozen block of rows, 1 for one updated without weight decay, 2 for one updated with it.
All inputs are finite; a program needn't handle non-finite values.
Results may differ from a plain program's by a relative error of at most 0.017.
Values may be sent and summed in bfloat16 or wider, within the bound.
No kernel may reach another device: no remote copies, remote signals or barrier semaphores. Data moves between devices by JAX's collectives and lax.ppermute only.
A program may use at most 128 MiB of HBM per device.

v0:
```python
import jax
import jax.numpy as jnp
from jax import lax
from jax.sharding import PartitionSpec as P

HEAD_DIM = 128
SPAN = 256
ROW_BLOCK = 32
NORM_EPS = 1e-06
BETA_ONE = 0.9
BETA_TWO = 0.95
ADAM_EPS = 1e-08
WEIGHT_DECAY = 0.1


def window_scan(gain, state, axis, sign):
    count = lax.axis_size(axis)
    place = lax.axis_index(axis)

    def join(near, far):
        return (near[0] * far[0], near[1] + near[0][:, None, None] * far[1])

    def fetch(value, step):
        pairs = [(i, i + sign * step) for i in range(count) if 0 <= i + sign * step < count]
        got = lax.ppermute(value, axis, pairs)
        source = place - sign * step
        present = (source >= 0) & (source < count)
        return jax.tree.map(lambda g, e: jnp.where(present, g, e), got, identity)

    own = (gain, state)
    identity = (jnp.ones_like(gain), jnp.zeros_like(state))
    near = [fetch(own, step) for step in (1, 2, 3)]
    inner = join(join(near[0], near[1]), near[2])
    window = join(own, inner)
    total = inner
    for step in (4, 8, 12):
        total = join(total, fetch(window, step))
    return total[1]


def decay_mask(cumul):
    along = jnp.swapaxes(cumul, 1, 2)
    spread = along[:, :, :, None] - along[:, :, None, :]
    length = cumul.shape[1]
    lower = jnp.tril(jnp.ones((length, length), jnp.float32))
    return jnp.exp(jnp.minimum(spread, 0.0)) * lower


def per_device(
    queries,
    keys,
    values,
    gate_pre,
    log_decay,
    out_grad,
    out_weight,
    moment_one,
    moment_two,
    group_ids,
    step_count,
):
    tok_local = queries.shape[1]
    head_local = log_decay.shape[2]
    width_local = queries.shape[2]
    blocks = tok_local // SPAN
    shaped = (blocks, SPAN, head_local, HEAD_DIM)
    query_c = queries.reshape(shaped)
    key_c = keys.reshape(shaped)
    value_c = values.reshape(shaped)
    cumul = jnp.cumsum(log_decay.reshape(blocks, SPAN, head_local), axis=1)
    totals = cumul[:, -1, :]
    masking = decay_mask(cumul)
    decay_in = jnp.exp(cumul)[..., None]
    decay_out = jnp.exp(totals[:, None, :] - cumul)[..., None]
    scores = jnp.einsum("cthe,cuhe->chtu", query_c, key_c, preferred_element_type=jnp.float32)
    probs = (scores * masking).astype(jnp.bfloat16)
    intra = jnp.einsum("chtu,cuhe->cthe", probs, value_c, preferred_element_type=jnp.float32)
    scaled = (decay_out * key_c).astype(jnp.bfloat16)
    updates = jnp.einsum("cthe,cthf->chef", scaled, value_c, preferred_element_type=jnp.float32)
    running = jnp.zeros((head_local, HEAD_DIM, HEAD_DIM), jnp.float32)
    leading = jnp.zeros((head_local,), jnp.float32)
    start_list = []
    lead_list = []
    for block in range(blocks):
        start_list.append(running)
        lead_list.append(leading)
        running = jnp.exp(totals[block])[:, None, None] * running + updates[block]
        leading = leading + totals[block]
    local_start = jnp.stack(start_list)
    lead_sums = jnp.stack(lead_list)
    incoming = window_scan(jnp.exp(leading), running, "ctx", 1)
    states = local_start + jnp.exp(lead_sums)[:, :, None, None] * incoming[None]
    rounded = states.astype(jnp.bfloat16)
    inter = decay_in * jnp.einsum(
        "cthe,chef->cthf", query_c, rounded, preferred_element_type=jnp.float32
    )
    attn = intra + inter
    square = jnp.mean(attn * attn, axis=-1, keepdims=True)
    inverse = lax.rsqrt(square + NORM_EPS)
    normed = attn * inverse
    silu_gate = jax.nn.silu(gate_pre.reshape(shaped).astype(jnp.float32))
    mixed = (normed * silu_gate).astype(jnp.bfloat16).reshape(tok_local, width_local)
    features = lax.all_gather(out_grad, "head", axis=2, tiled=True)[0]
    weight_b = out_weight.astype(jnp.bfloat16)
    columns = features
    mixed_grad = jnp.dot(
        columns,
        lax.all_gather(
            lax.all_gather(weight_b, "fsdp", axis=0, tiled=True), "ctx", axis=0, tiled=True
        ),
        preferred_element_type=jnp.float32,
    )
    columns = features
    grad_rows = lax.psum_scatter(
        lax.psum_scatter(
            jnp.einsum("td,th->dh", columns, mixed, preferred_element_type=jnp.float32).astype(
                jnp.bfloat16
            ),
            "ctx",
            scatter_dimension=0,
            tiled=True,
        ).astype(jnp.float32),
        "fsdp",
        scatter_dimension=0,
        tiled=True,
    )
    normed_grad = mixed_grad.reshape(shaped) * silu_gate
    inner = jnp.mean(normed_grad * normed, axis=-1, keepdims=True)
    attn_grad = (inverse * (normed_grad - normed * inner)).astype(jnp.bfloat16)
    inners = jnp.einsum("cthf,cuhf->chtu", attn_grad, value_c, preferred_element_type=jnp.float32)
    dprobs = (inners * masking).astype(jnp.bfloat16)
    qgrad = jnp.einsum("chtu,cuhe->cthe", dprobs, key_c, preferred_element_type=jnp.float32)
    kgrad = jnp.einsum("chtu,cthe->cuhe", dprobs, query_c, preferred_element_type=jnp.float32)
    vgrad = jnp.einsum("chtu,cthf->cuhf", probs, attn_grad, preferred_element_type=jnp.float32)
    weighted = (decay_in * query_c).astype(jnp.bfloat16)
    back_updates = jnp.einsum(
        "cthe,cthf->chef", weighted, attn_grad, preferred_element_type=jnp.float32
    )
    backing = jnp.zeros((head_local, HEAD_DIM, HEAD_DIM), jnp.float32)
    trailing = jnp.zeros((head_local,), jnp.float32)
    after_list = [None] * blocks
    trail_list = [None] * blocks
    for block in reversed(range(blocks)):
        after_list[block] = backing
        trail_list[block] = trailing
        backing = jnp.exp(totals[block])[:, None, None] * backing + back_updates[block]
        trailing = trailing + totals[block]
    local_after = jnp.stack(after_list)
    trail_sums = jnp.stack(trail_list)
    arriving = window_scan(jnp.exp(leading), backing, "ctx", -1)
    after_full = local_after + jnp.exp(trail_sums)[:, :, None, None] * arriving[None]
    back_b = after_full.astype(jnp.bfloat16)
    qgrad = qgrad + decay_in * jnp.einsum(
        "cthf,chef->cthe", attn_grad, rounded, preferred_element_type=jnp.float32
    )
    kgrad = kgrad + decay_out * jnp.einsum(
        "cuhf,chef->cuhe", value_c, back_b, preferred_element_type=jnp.float32
    )
    vgrad = vgrad + decay_out * jnp.einsum(
        "cuhe,chef->cuhf", key_c, back_b, preferred_element_type=jnp.float32
    )
    query_grad = qgrad.astype(jnp.bfloat16).reshape(1, tok_local, width_local)
    key_grad = kgrad.astype(jnp.bfloat16).reshape(1, tok_local, width_local)
    value_grad = vgrad.astype(jnp.bfloat16).reshape(1, tok_local, width_local)
    token_count = tok_local * lax.axis_size("ctx") * lax.axis_size("fsdp")
    grad = grad_rows / jnp.sqrt(jnp.float32(token_count))
    row_group = jnp.repeat(group_ids, ROW_BLOCK)[:, None]
    stepped = step_count[0].astype(jnp.float32)
    first = BETA_ONE * moment_one + (1.0 - BETA_ONE) * grad
    second = BETA_TWO * moment_two + (1.0 - BETA_TWO) * grad * grad
    correct_one = 1.0 - jnp.power(BETA_ONE, stepped)
    correct_two = 1.0 - jnp.power(BETA_TWO, stepped)
    active = row_group >= 1
    decayed = (row_group == 2).astype(jnp.float32)
    direction = (
        first / correct_one / (jnp.sqrt(second / correct_two) + ADAM_EPS)
        + WEIGHT_DECAY * decayed * out_weight
    )
    new_moment_one = jnp.where(active, first, moment_one)
    new_moment_two = jnp.where(active, second, moment_two)
    weight_step = jnp.where(active, direction, 0.0)
    return (query_grad, key_grad, value_grad, new_moment_one, new_moment_two, weight_step)


def solution(mesh):
    in_specs = (
        P("fsdp", "ctx", "head"),
        P("fsdp", "ctx", "head"),
        P("fsdp", "ctx", "head"),
        P("fsdp", "ctx", "head"),
        P("fsdp", "ctx", "head"),
        P("fsdp", "ctx", "head"),
        P(("ctx", "fsdp"), "head"),
        P(("ctx", "fsdp"), "head"),
        P(("ctx", "fsdp"), "head"),
        P(("ctx", "fsdp")),
        P(),
    )
    out_specs = (
        P("fsdp", "ctx", "head"),
        P("fsdp", "ctx", "head"),
        P("fsdp", "ctx", "head"),
        P(("ctx", "fsdp"), "head"),
        P(("ctx", "fsdp"), "head"),
        P(("ctx", "fsdp"), "head"),
    )
    return jax.shard_map(
        per_device, mesh=mesh, in_specs=in_specs, out_specs=out_specs, check_vma=False
    )
```

profile of v0, /device:TPU:4, one launch (start us, length us, event | category | flops | bytes accessed | tf_op | source)
XLA Modules:
  0.0 349.9 jit_solution(11883345295995269854)
XLA Ops:
  8.2 13.5 %all_gather.10 = bf16[256,512]{1,0:T(8,128)(2,1)} all-gather(bf16[64,512]{1,0:T(8,128)(2,1)S(1)} %convert_element_type.66), channel_id=1, replica_groups=mesh['ctx'=16,'fsdp'=4,'head'=4] {'fsdp'}, dimensions={0}, use_global_device_ids=true | all-gather | bytes 327680 | tf_op jit(solution)/shard_map/all_gather | solution.py:109
  23.3 2.4 reduce-window.6
  31.5 8.5 %collective-permute-start.4 = (f32[4,128,128]{2,1,0:T(8,128)}, f32[4,128,128]{2,1,0:T(8,128)}, u32[]{:S(2)}, u32[]{:S(2)}) collective-permute-start(f32[4,128,128]{2,1,0:T(8,128)} %fusion.28), channel_id=1, source_target_pairs={{0,48},{16,64},{32,80},{48,96},{64,112},{80,128},{96,144},{112,160... | collective-permute-start | bytes 786440 | tf_op jit(solution)/shard_map/ppermute | solution.py:25
  40.0 6.8 %collective-permute-start.2 = (f32[4,128,128]{2,1,0:T(8,128)}, f32[4,128,128]{2,1,0:T(8,128)}, u32[]{:S(2)}, u32[]{:S(2)}) collective-permute-start(f32[4,128,128]{2,1,0:T(8,128)} %fusion.28), channel_id=1, source_target_pairs={{0,32},{16,48},{32,64},{48,80},{64,96},{80,112},{96,128},{112,144}... | collective-permute-start | bytes 786440 | tf_op jit(solution)/shard_map/ppermute | solution.py:25
  46.8 3.8 %collective-permute-start = (f32[4,128,128]{2,1,0:T(8,128)}, f32[4,128,128]{2,1,0:T(8,128)}, u32[]{:S(2)}, u32[]{:S(2)}) collective-permute-start(f32[4,128,128]{2,1,0:T(8,128)} %fusion.28), channel_id=1, source_target_pairs={{0,16},{16,32},{32,48},{48,64},{64,80},{80,96},{96,112},{112,128},... | collective-permute-start | bytes 786440 | tf_op jit(solution)/shard_map/ppermute | solution.py:25
  54.7 7.1 %collective-permute-start.5 = (f32[4]{0:T(128)S(1)}, f32[4]{0:T(128)S(1)}, u32[]{:S(2)}, u32[]{:S(2)}) collective-permute-start(f32[4]{0:T(128)S(1)} %get-tuple-element.40), channel_id=1, source_target_pairs={{0,48},{16,64},{32,80},{48,96},{64,112},{80,128},{96,144},{112,160... | collective-permute-start | bytes 56 | tf_op jit(solution)/shard_map/ppermute | solution.py:25
  61.9 4.3 %collective-permute-start.3 = (f32[4]{0:T(128)S(1)}, f32[4]{0:T(128)S(1)}, u32[]{:S(2)}, u32[]{:S(2)}) collective-permute-start(f32[4]{0:T(128)S(1)} %get-tuple-element.40), channel_id=1, source_target_pairs={{0,32},{16,48},{32,64},{48,80},{64,96},{80,112},{96,128},{112,144}... | collective-permute-start | bytes 56 | tf_op jit(solution)/shard_map/ppermute | solution.py:25
  66.2 22.1 %collective-permute-done.5 = f32[4]{0:T(128)S(1)} collective-permute-done((f32[4]{0:T(128)S(1)}, f32[4]{0:T(128)S(1)}, u32[]{:S(2)}, u32[]{:S(2)}) %collective-permute-start.5) | collective-permute-done | bytes 48 | tf_op jit(solution)/shard_map/ppermute | solution.py:25
  88.3 4.0 %collective-permute-start.1 = (f32[4]{0:T(128)S(1)}, f32[4]{0:T(128)S(1)}, u32[]{:S(2)}, u32[]{:S(2)}) collective-permute-start(f32[4]{0:T(128)S(1)} %get-tuple-element.40), channel_id=1, source_target_pairs={{0,16},{16,32},{32,48},{48,64},{64,80},{80,96},{96,112},{112,128},... | collective-permute-start | bytes 56 | tf_op jit(solution)/shard_map/ppermute | solution.py:25
  94.6 13.3 %collective-permute-start.10 = (f32[4,128,128]{2,1,0:T(8,128)}, f32[4,128,128]{2,1,0:T(8,128)S(1)}, u32[]{:S(2)}, u32[]{:S(2)}) collective-permute-start(f32[4,128,128]{2,1,0:T(8,128)} %get-tuple-element.55), channel_id=1, source_target_pairs={{0,192},{16,208},{32,224},{48,240},{1,193},{17,209},{33,225},{49,2... | collective-permute-start | bytes 786440 | tf_op jit(solution)/shard_map/ppermute | solution.py:25
  107.9 3.0 collective-permute-start.8
  110.9 2.2 collective-permute-start.6
  113.1 2.4 reshape.180
  115.5 2.5 copy.192
  119.3 5.7 %collective-permute-start.7 = (f32[4]{0:T(128)S(1)}, f32[4]{0:T(128)S(1)}, u32[]{:S(2)}, u32[]{:S(2)}) collective-permute-start(f32[4]{0:T(128)S(1)} %get-tuple-element.64), channel_id=1, source_target_pairs={{0,64},{16,80},{32,96},{48,112},{64,128},{80,144},{96,160},{112,17... | collective-permute-start | bytes 56 | tf_op jit(solution)/shard_map/ppermute | solution.py:25
  125.0 8.0 %collective-permute-done.7 = f32[4]{0:T(128)S(1)} collective-permute-done((f32[4]{0:T(128)S(1)}, f32[4]{0:T(128)S(1)}, u32[]{:S(2)}, u32[]{:S(2)}) %collective-permute-start.7) | collective-permute-done | bytes 48 | tf_op jit(solution)/shard_map/ppermute | solution.py:25
  133.9 1.5 multiply_reduce_fusion.1
  135.4 3.5 all-gather.5.cloned.1.call-done
  138.9 6.5 %copy.190 = bf16[512,4096]{1,0:T(8,128)(2,1)} copy(bf16[512,4096]{0,1:T(8,128)(2,1)} %bitcast.113) | data formatting | bytes 8388608 | tf_op jit(solution)/shard_map/dot_general | solution.py:106
  145.4 33.7 %all-gather.3.cloned.1.call-done = bf16[1,512,4096]{2,1,0:T(8,128)(2,1)} async-done(((bf16[1,512,1024]{2,1,0:T(8,128)(2,1)}), bf16[1,512,4096]{2,1,0:T(8,128)(2,1)}) %all-gather.3.cloned.1.call-update) | async-done | bytes 4194320 | tf_op jit(solution)/shard_map/all_gather | solution.py:103
  179.1 6.3 %multiply_reduce_fusion = (f32[2,256,4]{1,2,0:T(4,128)S(1)}, f32[2,256,4,128]{1,3,2,0:T(8,128)S(1)}) fusion(f32[2,256,4,128]{1,3,2,0:T(8,128)} %get-tuple-element.69, f32[2,256,4]{1,2,0:T(4,128)S(1)} %add_rsqrt_fusion, f32[2,256,4,128]{1,3,2,0:T(8,128)S(1)} %copy-done.3, bf16[2,256,4096,1]{2,1,3,0:T(8,128)(2,1)} %bitcast.112, ...), kind=kOutput, calls=%fused_computation.29 | convolution fusion | flops 2149578752 | bytes 11550720 | tf_op jit(solution)/shard_map/dot_general | solution.py:106
  188.0 6.6 %fusion = bf16[4096,512]{0,1:T(8,128)(2,1)} fusion(bf16[1,512,4096]{2,1,0:T(8,128)(2,1)} %all-gather.3.cloned.1.call-done, bf16[64,8,4,128]{3,2,1,0:T(4,128)(2,1)S(1)} %bitcast.115), kind=kOutput, calls=%fused_computation.1 | convolution fusion | flops 2149580800 | bytes 8912896 | tf_op jit(solution)/shard_map/td,th->dh/dot_general | solution.py:116
  201.7 2.9 collective-permute-done.20
  204.6 5.2 %collective-permute-done.18 = f32[4]{0:T(128)S(1)} collective-permute-done((f32[4]{0:T(128)S(1)}, f32[4]{0:T(128)S(1)}, u32[]{:S(2)}, u32[]{:S(2)}) %collective-permute-start.18) | collective-permute-done | bytes 48 | tf_op jit(solution)/shard_map/ppermute | solution.py:25
  212.9 1.5 collective-permute-start.11
  214.4 1.6 multiply_convert_fusion
  217.6 1.5 convolution_bitcast_fusion.5
  219.5 20.3 %collective-permute-done.15 = f32[4,128,128]{2,1,0:T(8,128)S(1)} collective-permute-done((f32[4,128,128]{2,1,0:T(8,128)S(1)}, f32[4,128,128]{2,1,0:T(8,128)S(1)}, u32[]{:S(2)}, u32[]{:S(2)}) %collective-permute-start.15) | collective-permute-done | bytes 262176 | tf_op jit(solution)/shard_map/ppermute | solution.py:25
  246.9 68.4 %reduce-scatter.5.cloned.1.call-done = bf16[256,512]{0,1:T(8,128)(2,1)} async-done(((bf16[4096,512]{0,1:T(8,128)(2,1)}), bf16[256,512]{0,1:T(8,128)(2,1)}) %reduce-scatter.5.cloned.1.call-update) | async-done | bytes 262160 | tf_op jit(solution)/shard_map/reduce_scatter | solution.py:115
  315.3 1.9 copy.233
  318.7 1.7 fusion.12
  323.6 16.2 %reduce-scatter.7.cloned.1.call-done = f32[64,512]{1,0:T(8,128)} async-done(((f32[256,512]{1,0:T(8,128)}), f32[64,512]{1,0:T(8,128)}) %reduce-scatter.7.cloned.1.call-update) | async-done | bytes 131088
  (144 shorter events, 45.8 us)
Async XLA Ops:
  7.2 22.2 %copy-start.14 = (bf16[1,512,512]{2,1,0:T(8,128)(2,1)S(1)}, bf16[1,512,512]{2,1,0:T(8,128)(2,1)}, u32[]{:S(2)}) copy-start(bf16[1,512,512]{2,1,0:T(8,128)(2,1)} %param.13) | copy-start | bytes 1572868
  7.2 131.7 %all-gather.5.cloned.1.call-start = ((), (), s32[]{:S(2)}) async-start(), calls=%async_computation.3 | async-start | bytes 4456448 | tf_op jit(solution)/shard_map/all_gather | solution.py:108
  21.8 157.3 %all-gather.3.cloned.1.call-start = ((), (), s32[]{:S(2)}) async-start(), calls=%async_computation.2 | async-start | bytes 5242880 | tf_op jit(solution)/shard_map/all_gather | solution.py:103
  22.5 292.8 %reduce-scatter.5.cloned.1.call-start = ((), (), s32[]{:S(2)}) async-start(), calls=%async_computation.4 | async-start | bytes 4456448 | tf_op jit(solution)/shard_map/reduce_scatter | solution.py:115
  26.4 24.2 %copy-start.15 = (bf16[1,512,512]{2,1,0:T(8,128)(2,1)S(1)}, bf16[1,512,512]{2,1,0:T(8,128)(2,1)}, u32[]{:S(2)}) copy-start(bf16[1,512,512]{2,1,0:T(8,128)(2,1)} %param.11) | copy-start | bytes 1572868
  26.5 27.0 %collective-permute-start.16 = (f32[4]{0:T(128)S(1)}, f32[4]{0:T(128)S(1)}, u32[]{:S(2)}, u32[]{:S(2)}) collective-permute-start(f32[4]{0:T(128)S(1)} %get-tuple-element.40), channel_id=1, source_target_pairs={{48,0},{64,16},{80,32},{96,48},{112,64},{128,80},{144,96},{160,112... | collective-permute-start | bytes 56 | tf_op jit(solution)/shard_map/ppermute | solution.py:25
  27.9 26.8 %collective-permute-start.14 = (f32[4]{0:T(128)S(1)}, f32[4]{0:T(128)S(1)}, u32[]{:S(2)}, u32[]{:S(2)}) collective-permute-start(f32[4]{0:T(128)S(1)} %get-tuple-element.40), channel_id=1, source_target_pairs={{32,0},{48,16},{64,32},{80,48},{96,64},{112,80},{128,96},{144,112}... | collective-permute-start | bytes 56 | tf_op jit(solution)/shard_map/ppermute | solution.py:25
  31.5 62.0 %collective-permute-start.4 = (f32[4,128,128]{2,1,0:T(8,128)}, f32[4,128,128]{2,1,0:T(8,128)}, u32[]{:S(2)}, u32[]{:S(2)}) collective-permute-start(f32[4,128,128]{2,1,0:T(8,128)} %fusion.28), channel_id=1, source_target_pairs={{0,48},{16,64},{32,80},{48,96},{64,112},{80,128},{96,144},{112,160... | collective-permute-start | bytes 786440 | tf_op jit(solution)/shard_map/ppermute | solution.py:25
  40.0 53.5 %collective-permute-start.2 = (f32[4,128,128]{2,1,0:T(8,128)}, f32[4,128,128]{2,1,0:T(8,128)}, u32[]{:S(2)}, u32[]{:S(2)}) collective-permute-start(f32[4,128,128]{2,1,0:T(8,128)} %fusion.28), channel_id=1, source_target_pairs={{0,32},{16,48},{32,64},{48,80},{64,96},{80,112},{96,128},{112,144}... | collective-permute-start | bytes 786440 | tf_op jit(solution)/shard_map/ppermute | solution.py:25
  46.8 46.8 %collective-permute-start = (f32[4,128,128]{2,1,0:T(8,128)}, f32[4,128,128]{2,1,0:T(8,128)}, u32[]{:S(2)}, u32[]{:S(2)}) collective-permute-start(f32[4,128,128]{2,1,0:T(8,128)} %fusion.28), channel_id=1, source_target_pairs={{0,16},{16,32},{32,48},{48,64},{64,80},{80,96},{96,112},{112,128},... | collective-permute-start | bytes 786440 | tf_op jit(solution)/shard_map/ppermute | solution.py:25
  53.4 8.5 %collective-permute-start.12 = (f32[4]{0:T(128)S(1)}, f32[4]{0:T(128)S(1)}, u32[]{:S(2)}, u32[]{:S(2)}) collective-permute-start(f32[4]{0:T(128)S(1)} %get-tuple-element.40), channel_id=1, source_target_pairs={{16,0},{32,16},{48,32},{64,48},{80,64},{96,80},{112,96},{128,112},... | collective-permute-start | bytes 56 | tf_op jit(solution)/shard_map/ppermute | solution.py:25
  54.7 33.5 %collective-permute-start.5 = (f32[4]{0:T(128)S(1)}, f32[4]{0:T(128)S(1)}, u32[]{:S(2)}, u32[]{:S(2)}) collective-permute-start(f32[4]{0:T(128)S(1)} %get-tuple-element.40), channel_id=1, source_target_pairs={{0,48},{16,64},{32,80},{48,96},{64,112},{80,128},{96,144},{112,160... | collective-permute-start | bytes 56 | tf_op jit(solution)/shard_map/ppermute | solution.py:25
  61.9 30.4 %collective-permute-start.3 = (f32[4]{0:T(128)S(1)}, f32[4]{0:T(128)S(1)}, u32[]{:S(2)}, u32[]{:S(2)}) collective-permute-start(f32[4]{0:T(128)S(1)} %get-tuple-element.40), channel_id=1, source_target_pairs={{0,32},{16,48},{32,64},{48,80},{64,96},{80,112},{96,128},{112,144}... | collective-permute-start | bytes 56 | tf_op jit(solution)/shard_map/ppermute | solution.py:25
  88.3 5.3 %collective-permute-start.1 = (f32[4]{0:T(128)S(1)}, f32[4]{0:T(128)S(1)}, u32[]{:S(2)}, u32[]{:S(2)}) collective-permute-start(f32[4]{0:T(128)S(1)} %get-tuple-element.40), channel_id=1, source_target_pairs={{0,16},{16,32},{32,48},{48,64},{64,80},{80,96},{96,112},{112,128},... | collective-permute-start | bytes 56 | tf_op jit(solution)/shard_map/ppermute | solution.py:25
  94.6 39.2 %copy-start.7 = (f32[4,128,128]{2,1,0:T(8,128)S(1)}, f32[4,128,128]{2,1,0:T(8,128)}, u32[]{:S(2)}) copy-start(f32[4,128,128]{2,1,0:T(8,128)} %get-tuple-element.56) | copy-start | bytes 786436
  94.6 38.5 %collective-permute-start.10 = (f32[4,128,128]{2,1,0:T(8,128)}, f32[4,128,128]{2,1,0:T(8,128)S(1)}, u32[]{:S(2)}, u32[]{:S(2)}) collective-permute-start(f32[4,128,128]{2,1,0:T(8,128)} %get-tuple-element.55), channel_id=1, source_target_pairs={{0,192},{16,208},{32,224},{48,240},{1,193},{17,209},{33,225},{49,2... | collective-permute-start | bytes 786440 | tf_op jit(solution)/shard_map/ppermute | solution.py:25
  107.9 25.1 %collective-permute-start.8 = (f32[4,128,128]{2,1,0:T(8,128)}, f32[4,128,128]{2,1,0:T(8,128)}, u32[]{:S(2)}, u32[]{:S(2)}) collective-permute-start(f32[4,128,128]{2,1,0:T(8,128)} %get-tuple-element.55), channel_id=1, source_target_pairs={{0,128},{16,144},{32,160},{48,176},{64,192},{80,208},{96,224},{112... | collective-permute-start | bytes 786440 | tf_op jit(solution)/shard_map/ppermute | solution.py:25
  110.9 22.2 %collective-permute-start.6 = (f32[4,128,128]{2,1,0:T(8,128)}, f32[4,128,128]{2,1,0:T(8,128)}, u32[]{:S(2)}, u32[]{:S(2)}) collective-permute-start(f32[4,128,128]{2,1,0:T(8,128)} %get-tuple-element.55), channel_id=1, source_target_pairs={{0,64},{16,80},{32,96},{48,112},{64,128},{80,144},{96,160},{112,17... | collective-permute-start | bytes 786440 | tf_op jit(solution)/shard_map/ppermute | solution.py:25
  118.1 7.0 %collective-permute-start.9 = (f32[4]{0:T(128)S(1)}, f32[4]{0:T(128)S(1)}, u32[]{:S(2)}, u32[]{:S(2)}) collective-permute-start(f32[4]{0:T(128)S(1)} %get-tuple-element.64), channel_id=1, source_target_pairs={{0,128},{16,144},{32,160},{48,176},{64,192},{80,208},{96,224},{112... | collective-permute-start | bytes 56 | tf_op jit(solution)/shard_map/ppermute | solution.py:25
  119.3 13.7 %collective-permute-start.7 = (f32[4]{0:T(128)S(1)}, f32[4]{0:T(128)S(1)}, u32[]{:S(2)}, u32[]{:S(2)}) collective-permute-start(f32[4]{0:T(128)S(1)} %get-tuple-element.64), channel_id=1, source_target_pairs={{0,64},{16,80},{32,96},{48,112},{64,128},{80,144},{96,160},{112,17... | collective-permute-start | bytes 56 | tf_op jit(solution)/shard_map/ppermute | solution.py:25
  138.9 40.2 %copy-start.3 = (f32[2,256,4,128]{1,3,2,0:T(8,128)S(1)}, f32[2,256,4,128]{1,3,2,0:T(8,128)}, u32[]{:S(2)}) copy-start(f32[2,256,4,128]{1,3,2,0:T(8,128)} %copy.192) | copy-start | bytes 3145732
  194.6 145.1 %reduce-scatter.7.cloned.1.call-start = ((), (), s32[]{:S(2)}) async-start(), calls=%async_computation.5 | async-start | bytes 655360
  199.1 5.5 %collective-permute-start.20 = (f32[4]{0:T(128)S(1)}, f32[4]{0:T(128)S(1)}, u32[]{:S(2)}, u32[]{:S(2)}) collective-permute-start(f32[4]{0:T(128)S(1)} %get-tuple-element.43), channel_id=1, source_target_pairs={{128,0},{144,16},{160,32},{176,48},{192,64},{208,80},{224,96},{240... | collective-permute-start | bytes 56 | tf_op jit(solution)/shard_map/ppermute | solution.py:25
  200.4 9.4 %collective-permute-start.18 = (f32[4]{0:T(128)S(1)}, f32[4]{0:T(128)S(1)}, u32[]{:S(2)}, u32[]{:S(2)}) collective-permute-start(f32[4]{0:T(128)S(1)} %get-tuple-element.43), channel_id=1, source_target_pairs={{64,0},{80,16},{96,32},{112,48},{128,64},{144,80},{160,96},{176,11... | collective-permute-start | bytes 56 | tf_op jit(solution)/shard_map/ppermute | solution.py:25
  210.2 29.6 %collective-permute-start.15 = (f32[4,128,128]{2,1,0:T(8,128)S(1)}, f32[4,128,128]{2,1,0:T(8,128)S(1)}, u32[]{:S(2)}, u32[]{:S(2)}) collective-permute-start(f32[4,128,128]{2,1,0:T(8,128)S(1)} %fusion.27), channel_id=1, source_target_pairs={{48,0},{64,16},{80,32},{96,48},{112,64},{128,80},{144,96},{160,112... | collective-permute-start | bytes 786440 | tf_op jit(solution)/shard_map/ppermute | solution.py:25
  211.6 28.7 %collective-permute-start.13 = (f32[4,128,128]{2,1,0:T(8,128)S(1)}, f32[4,128,128]{2,1,0:T(8,128)S(1)}, u32[]{:S(2)}, u32[]{:S(2)}) collective-permute-start(f32[4,128,128]{2,1,0:T(8,128)S(1)} %fusion.27), channel_id=1, source_target_pairs={{32,0},{48,16},{64,32},{80,48},{96,64},{112,80},{128,96},{144,112}... | collective-permute-start | bytes 786440 | tf_op jit(solution)/shard_map/ppermute | solution.py:25
  212.9 27.5 %collective-permute-start.11 = (f32[4,128,128]{2,1,0:T(8,128)S(1)}, f32[4,128,128]{2,1,0:T(8,128)S(1)}, u32[]{:S(2)}, u32[]{:S(2)}) collective-permute-start(f32[4,128,128]{2,1,0:T(8,128)S(1)} %fusion.27), channel_id=1, source_target_pairs={{16,0},{32,16},{48,32},{64,48},{80,64},{96,80},{112,96},{128,112},... | collective-permute-start | bytes 786440 | tf_op jit(solution)/shard_map/ppermute | solution.py:25
  219.0 26.2 %copy-start.6 = (f32[4,128,128]{2,1,0:T(8,128)S(1)}, f32[4,128,128]{2,1,0:T(8,128)}, u32[]{:S(2)}) copy-start(f32[4,128,128]{2,1,0:T(8,128)} %copy-done.5) | copy-start | bytes 786436
  241.4 76.0 %collective-permute-start.21 = (f32[4,128,128]{2,1,0:T(8,128)}, f32[4,128,128]{2,1,0:T(8,128)}, u32[]{:S(2)}, u32[]{:S(2)}) collective-permute-start(f32[4,128,128]{2,1,0:T(8,128)} %get-tuple-element.47), channel_id=1, source_target_pairs={{192,0},{208,16},{224,32},{240,48},{193,1},{209,17},{225,33},{241,... | collective-permute-start | bytes 786440 | tf_op jit(solution)/shard_map/ppermute | solution.py:25
  242.6 74.7 %collective-permute-start.19 = (f32[4,128,128]{2,1,0:T(8,128)}, f32[4,128,128]{2,1,0:T(8,128)}, u32[]{:S(2)}, u32[]{:S(2)}) collective-permute-start(f32[4,128,128]{2,1,0:T(8,128)} %get-tuple-element.47), channel_id=1, source_target_pairs={{128,0},{144,16},{160,32},{176,48},{192,64},{208,80},{224,96},{240... | collective-permute-start | bytes 786440 | tf_op jit(solution)/shard_map/ppermute | solution.py:25
  243.9 73.4 %collective-permute-start.17 = (f32[4,128,128]{2,1,0:T(8,128)}, f32[4,128,128]{2,1,0:T(8,128)}, u32[]{:S(2)}, u32[]{:S(2)}) collective-permute-start(f32[4,128,128]{2,1,0:T(8,128)} %get-tuple-element.47), channel_id=1, source_target_pairs={{64,0},{80,16},{96,32},{112,48},{128,64},{144,80},{160,96},{176,11... | collective-permute-start | bytes 786440 | tf_op jit(solution)/shard_map/ppermute | solution.py:25
  245.6 71.8 %copy-start.8 = (f32[4,128,128]{2,1,0:T(8,128)S(1)}, f32[4,128,128]{2,1,0:T(8,128)}, u32[]{:S(2)}) copy-start(f32[4,128,128]{2,1,0:T(8,128)} %get-tuple-element.48) | copy-start | bytes 786436
  (15 other events, 113.3 us)
Sparse Core Ops, SparseCore 0:
  21.9 116.9 all-gather.4
  140.7 38.3 all-gather.2
  194.7 120.5 reduce-scatter.4
  317.7 21.9 reduce-scatter.6
where the time goes:
time: 351 us; the launch traced here: 350 us
  waiting for transfers between devices  183 us (52%)
  starting transfers between devices  74.7 us (21%)
  local copies, waits for them, and re-layouts  29.4 us (8%)
  matrix products  24.4 us (7%)
  between operations  15.2 us (4%)
  blocking collectives  13.5 us (4%)
  other arithmetic  9.79 us (3%)
    ppermute x22, starting transfers between devices, fetch(): got = lax.ppermute(value, axis, pairs)  74.6 us
    reduce_scatter x1, waiting for transfers between devices, per_device(): lax.psum_scatter(jnp.einsum('td,th->dh', columns, mixed, preferred_elemen...  68.4 us
    ppermute x22, waiting for transfers between devices, fetch(): got = lax.ppermute(value, axis, pairs)  60.4 us
    all_gather x1, waiting for transfers between devices, per_device(): features = lax.all_gather(out_grad, 'head', axis=2, tiled=True)[0]  33.7 us
    unnamed x5, waiting for transfers between devices  16.9 us
    all_gather x1, blocking collectives, per_device(): lax.all_gather(weight_b, 'fsdp', axis=0, tiled=True)  13.5 us
    unnamed x50, local copies, waits for them, and re-layouts  10.3 us
  transfers between devices with their start and end apart: 26, of which 11 were waited for; matrix products, arithmetic and copies ran while one was open for 12% of the time, Pallas kernels for 0%

commit v1 on v0

--- a/solution.py
+++ b/solution.py
@@ -11,6 +11,27 @@
 BETA_TWO = 0.95
 ADAM_EPS = 1e-08
 WEIGHT_DECAY = 0.1
+
+
+def ring_gather(value, axis, dim):
+    size, index, rows = (lax.axis_size(axis), lax.axis_index(axis), value.shape[dim])
+    right = [(i, (i + 1) % size) for i in range(size)]
+    left = [(i, (i - 1) % size) for i in range(size)]
+    filled = jnp.zeros((*value.shape[:dim], size * rows, *value.shape[dim + 1 :]), value.dtype)
+    filled = lax.dynamic_update_slice_in_dim(filled, value, index * rows, axis=dim)
+    from_left = from_right = value
+    halfway = size // 2
+    for step in range(1, halfway + 1):
+        from_left = lax.ppermute(from_left, axis, right)
+        filled = lax.dynamic_update_slice_in_dim(
+            filled, from_left, (index - step) % size * rows, axis=dim
+        )
+        if step < size - halfway:
+            from_right = lax.ppermute(from_right, axis, left)
+            filled = lax.dynamic_update_slice_in_dim(
+                filled, from_right, (index + step) % size * rows, axis=dim
+            )
+    return filled
 
 
 def window_scan(gain, state, axis, sign):
@@ -105,9 +126,7 @@
     columns = features
     mixed_grad = jnp.dot(
         columns,
-        lax.all_gather(
-            lax.all_gather(weight_b, "fsdp", axis=0, tiled=True), "ctx", axis=0, tiled=True
-        ),
+        lax.all_gather(ring_gather(weight_b, "fsdp", 0), "ctx", axis=0, tiled=True),
         preferred_element_type=jnp.float32,
     )
     columns = features

time: 351 us -> 320 us (0.912)
  waiting for transfers between devices: 183 us -> 169 us
  blocking collectives: 13.5 us -> 0 us
  local copies, waits for them, and re-layouts: 29.4 us -> 19.5 us
  starting transfers between devices: 74.7 us -> 80.5 us
    all_gather x1, waiting for transfers between devices: 33.7 us -> 0.02 us  [per_device(): features = lax.all_gather(out_grad, 'head', axis=2, tiled=True)[0]]
    all_gather x1, waiting for transfers between devices: 3.49 us -> 27.7 us  [per_device(): lax.all_gather(ring_gather(weight_b, 'fsdp', 0), 'ctx', axis=0, tiled=True)]
    all_gather x1 -> x0, blocking collectives: 13.5 us -> none  [per_device(): lax.all_gather(weight_b, 'fsdp', axis=0, tiled=True)]
    ppermute x22, waiting for transfers between devices: 60.4 us -> 49.9 us  [fetch(): got = lax.ppermute(value, axis, pairs)]
    ppermute x0 -> x3, waiting for transfers between devices: none -> 7.31 us  [the longest x2 7.31 us: ring_gather(): from_left = lax.ppermute(from_left, axis, right)]
    dot_general x1 -> x0, local copies, waits for them, and re-layouts: 6.49 us -> none  [per_device(): jnp.dot(columns, lax.all_gather(lax.all_gather(weight_b, 'fsdp', axis=0,...]
    convert_element_type x2, local copies, waits for them, and re-layouts: 4.97 us -> 0.68 us  [per_device(): silu_gate = jax.nn.silu(gate_pre.reshape(shaped).astype(jnp.float32))]
    reduce_scatter x1, waiting for transfers between devices: 68.4 us -> 64.2 us  [per_device(): lax.psum_scatter(jnp.einsum('td,th->dh', columns, mixed, preferred_elemen...]
  transfers between devices with their start and end apart: 26 -> 29, of which waited for: 11 -> 12; matrix products, arithmetic and copies ran while one was open for 12% -> 10% of each run, Pallas kernels for 0% -> 0%
where the time goes in v1:
time: 320 us; the launch traced here: 319 us
  waiting for transfers between devices  169 us (53%)
  starting transfers between devices  80.5 us (25%)
  matrix products  25.3 us (8%)
  local copies, waits for them, and re-layouts  19.5 us (6%)
  between operations  15.3 us (5%)
  other arithmetic  10.2 us (3%)
    ppermute x22, starting transfers between devices, fetch(): got = lax.ppermute(value, axis, pairs)  76.6 us
    reduce_scatter x1, waiting for transfers between devices, per_device(): lax.psum_scatter(jnp.einsum('td,th->dh', columns, mixed, preferred_elemen...  64.2 us
    ppermute x22, waiting for transfers between devices, fetch(): got = lax.ppermute(value, axis, pairs)  49.9 us
    all_gather x1, waiting for transfers between devices, per_device(): lax.all_gather(ring_gather(weight_b, 'fsdp', 0), 'ctx', axis=0, tiled=True)  27.7 us
    unnamed x5, waiting for transfers between devices  19.4 us
    unnamed x66, local copies, waits for them, and re-layouts  10 us
    ppermute x2, waiting for transfers between devices, ring_gather(): from_left = lax.ppermute(from_left, axis, right)  7.31 us
    dot_general x1, matrix products, per_device(): jnp.dot(columns, lax.all_gather(ring_gather(weight_b, 'fsdp', 0), 'ctx',...  6.83 us
  transfers between devices with their start and end apart: 29, of which 12 were waited for; matrix products, arithmetic and copies ran while one was open for 10% of the time, Pallas kernels for 0%

profile of v1, /device:TPU:4, one launch (start us, length us, event | category | flops | bytes accessed | tf_op | source)
XLA Modules:
  0.0 319.4 jit_solution(17071280351191995608)
XLA Ops:
  8.9 1.7 collective-permute-start.11
  10.6 1.7 collective-permute-start.12
  12.3 2.2 collective-permute-done.11
  14.9 5.1 %collective-permute-done.13 = bf16[64,512]{1,0:T(8,128)(2,1)S(1)} collective-permute-done((bf16[64,512]{1,0:T(8,128)(2,1)S(1)}, bf16[64,512]{1,0:T(8,128)(2,1)S(1)}, u32[]{:S(2)}, u32[]{:S(2)}) %collective-permute-start.13) | collective-permute-done | bytes 65568 | tf_op jit(solution)/shard_map/ppermute | solution.py:25
  20.8 2.4 reduce-window.6
  29.1 8.5 %collective-permute-start.4 = (f32[4,128,128]{2,1,0:T(8,128)}, f32[4,128,128]{2,1,0:T(8,128)}, u32[]{:S(2)}, u32[]{:S(2)}) collective-permute-start(f32[4,128,128]{2,1,0:T(8,128)} %fusion.33), channel_id=1, source_target_pairs={{0,48},{16,64},{32,80},{48,96},{64,112},{80,128},{96,144},{112,160... | collective-permute-start | bytes 786440 | tf_op jit(solution)/shard_map/ppermute | solution.py:46
  37.5 6.7 %collective-permute-start.2 = (f32[4,128,128]{2,1,0:T(8,128)}, f32[4,128,128]{2,1,0:T(8,128)}, u32[]{:S(2)}, u32[]{:S(2)}) collective-permute-start(f32[4,128,128]{2,1,0:T(8,128)} %fusion.33), channel_id=1, source_target_pairs={{0,32},{16,48},{32,64},{48,80},{64,96},{80,112},{96,128},{112,144}... | collective-permute-start | bytes 786440 | tf_op jit(solution)/shard_map/ppermute | solution.py:46
  44.3 3.9 %collective-permute-start = (f32[4,128,128]{2,1,0:T(8,128)}, f32[4,128,128]{2,1,0:T(8,128)}, u32[]{:S(2)}, u32[]{:S(2)}) collective-permute-start(f32[4,128,128]{2,1,0:T(8,128)} %fusion.33), channel_id=1, source_target_pairs={{0,16},{16,32},{32,48},{48,64},{64,80},{80,96},{96,112},{112,128},... | collective-permute-start | bytes 786440 | tf_op jit(solution)/shard_map/ppermute | solution.py:46
  52.3 7.1 %collective-permute-start.5 = (f32[4]{0:T(128)S(1)}, f32[4]{0:T(128)S(1)}, u32[]{:S(2)}, u32[]{:S(2)}) collective-permute-start(f32[4]{0:T(128)S(1)} %get-tuple-element.40), channel_id=1, source_target_pairs={{0,48},{16,64},{32,80},{48,96},{64,112},{80,128},{96,144},{112,160... | collective-permute-start | bytes 56 | tf_op jit(solution)/shard_map/ppermute | solution.py:46
  59.4 4.3 %collective-permute-start.3 = (f32[4]{0:T(128)S(1)}, f32[4]{0:T(128)S(1)}, u32[]{:S(2)}, u32[]{:S(2)}) collective-permute-start(f32[4]{0:T(128)S(1)} %get-tuple-element.40), channel_id=1, source_target_pairs={{0,32},{16,48},{32,64},{48,80},{64,96},{80,112},{96,128},{112,144}... | collective-permute-start | bytes 56 | tf_op jit(solution)/shard_map/ppermute | solution.py:46
  63.7 6.3 %collective-permute-done.5 = f32[4]{0:T(128)S(1)} collective-permute-done((f32[4]{0:T(128)S(1)}, f32[4]{0:T(128)S(1)}, u32[]{:S(2)}, u32[]{:S(2)}) %collective-permute-start.5) | collective-permute-done | bytes 48 | tf_op jit(solution)/shard_map/ppermute | solution.py:46
  70.0 3.6 %collective-permute-start.1 = (f32[4]{0:T(128)S(1)}, f32[4]{0:T(128)S(1)}, u32[]{:S(2)}, u32[]{:S(2)}) collective-permute-start(f32[4]{0:T(128)S(1)} %get-tuple-element.40), channel_id=1, source_target_pairs={{0,16},{16,32},{32,48},{48,64},{64,80},{80,96},{96,112},{112,128},... | collective-permute-start | bytes 56 | tf_op jit(solution)/shard_map/ppermute | solution.py:46
  75.9 17.3 %collective-permute-start.10 = (f32[4,128,128]{2,1,0:T(8,128)}, f32[4,128,128]{2,1,0:T(8,128)S(1)}, u32[]{:S(2)}, u32[]{:S(2)}) collective-permute-start(f32[4,128,128]{2,1,0:T(8,128)} %get-tuple-element.57), channel_id=1, source_target_pairs={{0,192},{16,208},{32,224},{48,240},{1,193},{17,209},{33,225},{49,2... | collective-permute-start | bytes 786440 | tf_op jit(solution)/shard_map/ppermute | solution.py:46
  93.2 2.0 collective-permute-start.8
  95.2 3.2 collective-permute-start.6
  100.4 4.0 %collective-permute-start.7 = (f32[4]{0:T(128)S(1)}, f32[4]{0:T(128)S(1)}, u32[]{:S(2)}, u32[]{:S(2)}) collective-permute-start(f32[4]{0:T(128)S(1)} %get-tuple-element.66), channel_id=1, source_target_pairs={{0,64},{16,80},{32,96},{48,112},{64,128},{80,144},{96,160},{112,17... | collective-permute-start | bytes 56 | tf_op jit(solution)/shard_map/ppermute | solution.py:46
  104.5 4.1 %collective-permute-done.9 = f32[4]{0:T(128)S(1)} collective-permute-done((f32[4]{0:T(128)S(1)}, f32[4]{0:T(128)S(1)}, u32[]{:S(2)}, u32[]{:S(2)}) %collective-permute-start.9) | collective-permute-done | bytes 48 | tf_op jit(solution)/shard_map/ppermute | solution.py:46
  108.6 10.0 %collective-permute-done.7 = f32[4]{0:T(128)S(1)} collective-permute-done((f32[4]{0:T(128)S(1)}, f32[4]{0:T(128)S(1)}, u32[]{:S(2)}, u32[]{:S(2)}) %collective-permute-start.7) | collective-permute-done | bytes 48 | tf_op jit(solution)/shard_map/ppermute | solution.py:46
  119.5 1.8 multiply_reduce_fusion.1
  121.4 27.7 %all-gather.3.cloned.1.call-done = bf16[4096,512]{1,0:T(8,128)(2,1)} async-done(((bf16[256,512]{1,0:T(8,128)(2,1)}), bf16[4096,512]{1,0:T(8,128)(2,1)}) %all-gather.3.cloned.1.call-update) | async-done | bytes 4194320 | tf_op jit(solution)/shard_map/all_gather | solution.py:129
  149.1 6.8 %fusion.4 = f32[512,512]{0,1:T(8,128)} fusion(bf16[4096,512]{1,0:T(8,128)(2,1)} %all-gather.3.cloned.1.call-done, bf16[1,512,4096]{2,1,0:T(8,128)(2,1)} %all-gather.5.cloned.1.call-done), kind=kOutput, calls=%fused_computation.8 | convolution fusion | flops 2147483648 | bytes 9437184 | tf_op jit(solution)/shard_map/dot_general | solution.py:127
  155.9 1.9 reshape.182
  160.9 6.6 %fusion = bf16[4096,512]{0,1:T(8,128)(2,1)} fusion(bf16[1,512,4096]{2,1,0:T(8,128)(2,1)} %all-gather.5.cloned.1.call-done, bf16[64,8,4,128]{3,2,1,0:T(4,128)(2,1)S(1)} %bitcast.110), kind=kOutput, calls=%fused_computation.1 | convolution fusion | flops 2149580800 | bytes 8912896 | tf_op jit(solution)/shard_map/td,th->dh/dot_general | solution.py:135
  174.7 2.9 collective-permute-done.23
  177.5 5.2 %collective-permute-done.21 = f32[4]{0:T(128)S(1)} collective-permute-done((f32[4]{0:T(128)S(1)}, f32[4]{0:T(128)S(1)}, u32[]{:S(2)}, u32[]{:S(2)}) %collective-permute-start.21) | collective-permute-done | bytes 48 | tf_op jit(solution)/shard_map/ppermute | solution.py:46
  189.4 1.5 convolution_bitcast_fusion.5
  191.4 20.1 %collective-permute-done.18 = f32[4,128,128]{2,1,0:T(8,128)S(1)} collective-permute-done((f32[4,128,128]{2,1,0:T(8,128)S(1)}, f32[4,128,128]{2,1,0:T(8,128)S(1)}, u32[]{:S(2)}, u32[]{:S(2)}) %collective-permute-start.18) | collective-permute-done | bytes 262176 | tf_op jit(solution)/shard_map/ppermute | solution.py:46
  214.9 1.5 collective-permute-start.20
  218.1 64.2 %reduce-scatter.5.cloned.1.call-done = bf16[256,512]{0,1:T(8,128)(2,1)} async-done(((bf16[4096,512]{0,1:T(8,128)(2,1)}), bf16[256,512]{0,1:T(8,128)(2,1)}) %reduce-scatter.5.cloned.1.call-update) | async-done | bytes 262160 | tf_op jit(solution)/shard_map/reduce_scatter | solution.py:134
  282.3 1.9 copy.237
  285.6 1.7 fusion.17
  290.5 18.7 %reduce-scatter.7.cloned.1.call-done = f32[64,512]{1,0:T(8,128)} async-done(((f32[256,512]{1,0:T(8,128)}), f32[64,512]{1,0:T(8,128)}) %reduce-scatter.7.cloned.1.call-update) | async-done | bytes 131088
  (170 shorter events, 47.4 us)
Async XLA Ops:
  7.2 114.2 %all-gather.5.cloned.1.call-start = ((), (), s32[]{:S(2)}) async-start(), calls=%async_computation.3 | async-start | bytes 5242880 | tf_op jit(solution)/shard_map/all_gather | solution.py:124
  7.9 141.2 %all-gather.3.cloned.1.call-start = ((), (), s32[]{:S(2)}) async-start(), calls=%async_computation.2 | async-start | bytes 4456448 | tf_op jit(solution)/shard_map/all_gather | solution.py:129
  8.9 5.6 %collective-permute-start.11 = (bf16[64,512]{1,0:T(8,128)(2,1)S(1)}, bf16[64,512]{1,0:T(8,128)(2,1)S(1)}, u32[]{:S(2)}, u32[]{:S(2)}) collective-permute-start(bf16[64,512]{1,0:T(8,128)(2,1)S(1)} %get-tuple-element.50), channel_id=1, source_target_pairs={{0,4},{4,8},{8,12},{12,0},{1,5},{5,9},{9,13},{13,1},{2,6},{6,10},{... | collective-permute-start | bytes 196616 | tf_op jit(solution)/shard_map/ppermute | solution.py:25
  10.6 4.3 %collective-permute-start.12 = (bf16[64,512]{1,0:T(8,128)(2,1)S(1)}, bf16[64,512]{1,0:T(8,128)(2,1)S(1)}, u32[]{:S(2)}, u32[]{:S(2)}) collective-permute-start(bf16[64,512]{1,0:T(8,128)(2,1)S(1)} %get-tuple-element.50), channel_id=1, source_target_pairs={{0,12},{4,0},{8,4},{12,8},{1,13},{5,1},{9,5},{13,9},{2,14},{6,2},{... | collective-permute-start | bytes 196616 | tf_op jit(solution)/shard_map/ppermute | solution.py:30
  14.5 5.5 %collective-permute-start.13 = (bf16[64,512]{1,0:T(8,128)(2,1)S(1)}, bf16[64,512]{1,0:T(8,128)(2,1)S(1)}, u32[]{:S(2)}, u32[]{:S(2)}) collective-permute-start(bf16[64,512]{1,0:T(8,128)(2,1)S(1)} %collective-permute-done.11), channel_id=1, source_target_pairs={{0,4},{4,8},{8,12},{12,0},{1,5},{5,9},{9,13},{13,1},{2,6},{6,10},{... | collective-permute-start | bytes 196616 | tf_op jit(solution)/shard_map/ppermute | solution.py:25
  20.7 261.6 %reduce-scatter.5.cloned.1.call-start = ((), (), s32[]{:S(2)}) async-start(), calls=%async_computation.4 | async-start | bytes 4456448 | tf_op jit(solution)/shard_map/reduce_scatter | solution.py:134
  24.0 27.0 %collective-permute-start.19 = (f32[4]{0:T(128)S(1)}, f32[4]{0:T(128)S(1)}, u32[]{:S(2)}, u32[]{:S(2)}) collective-permute-start(f32[4]{0:T(128)S(1)} %get-tuple-element.40), channel_id=1, source_target_pairs={{48,0},{64,16},{80,32},{96,48},{112,64},{128,80},{144,96},{160,112... | collective-permute-start | bytes 56 | tf_op jit(solution)/shard_map/ppermute | solution.py:46
  25.4 26.9 %collective-permute-start.17 = (f32[4]{0:T(128)S(1)}, f32[4]{0:T(128)S(1)}, u32[]{:S(2)}, u32[]{:S(2)}) collective-permute-start(f32[4]{0:T(128)S(1)} %get-tuple-element.40), channel_id=1, source_target_pairs={{32,0},{48,16},{64,32},{80,48},{96,64},{112,80},{128,96},{144,112}... | collective-permute-start | bytes 56 | tf_op jit(solution)/shard_map/ppermute | solution.py:46
  29.1 45.9 %collective-permute-start.4 = (f32[4,128,128]{2,1,0:T(8,128)}, f32[4,128,128]{2,1,0:T(8,128)}, u32[]{:S(2)}, u32[]{:S(2)}) collective-permute-start(f32[4,128,128]{2,1,0:T(8,128)} %fusion.33), channel_id=1, source_target_pairs={{0,48},{16,64},{32,80},{48,96},{64,112},{80,128},{96,144},{112,160... | collective-permute-start | bytes 786440 | tf_op jit(solution)/shard_map/ppermute | solution.py:46
  37.5 37.4 %collective-permute-start.2 = (f32[4,128,128]{2,1,0:T(8,128)}, f32[4,128,128]{2,1,0:T(8,128)}, u32[]{:S(2)}, u32[]{:S(2)}) collective-permute-start(f32[4,128,128]{2,1,0:T(8,128)} %fusion.33), channel_id=1, source_target_pairs={{0,32},{16,48},{32,64},{48,80},{64,96},{80,112},{96,128},{112,144}... | collective-permute-start | bytes 786440 | tf_op jit(solution)/shard_map/ppermute | solution.py:46
  44.3 30.6 %collective-permute-start = (f32[4,128,128]{2,1,0:T(8,128)}, f32[4,128,128]{2,1,0:T(8,128)}, u32[]{:S(2)}, u32[]{:S(2)}) collective-permute-start(f32[4,128,128]{2,1,0:T(8,128)} %fusion.33), channel_id=1, source_target_pairs={{0,16},{16,32},{32,48},{48,64},{64,80},{80,96},{96,112},{112,128},... | collective-permute-start | bytes 786440 | tf_op jit(solution)/shard_map/ppermute | solution.py:46
  48.6 71.0 %copy-start = (bf16[2,256,4,128]{1,3,2,0:T(8,128)(2,1)}, bf16[2,256,4,128]{1,3,2,0:T(8,128)(2,1)S(1)}, u32[]{:S(2)}) copy-start(bf16[2,256,4,128]{1,3,2,0:T(8,128)(2,1)S(1)} %copy.204) | copy-start | bytes 1572868
  49.4 49.1 %copy-start.17 = (bf16[1,512,512]{2,1,0:T(8,128)(2,1)S(1)}, bf16[1,512,512]{2,1,0:T(8,128)(2,1)}, u32[]{:S(2)}) copy-start(bf16[1,512,512]{2,1,0:T(8,128)(2,1)} %param.14) | copy-start | bytes 1572868
  51.0 8.5 %collective-permute-start.15 = (f32[4]{0:T(128)S(1)}, f32[4]{0:T(128)S(1)}, u32[]{:S(2)}, u32[]{:S(2)}) collective-permute-start(f32[4]{0:T(128)S(1)} %get-tuple-element.40), channel_id=1, source_target_pairs={{16,0},{32,16},{48,32},{64,48},{80,64},{96,80},{112,96},{128,112},... | collective-permute-start | bytes 56 | tf_op jit(solution)/shard_map/ppermute | solution.py:46
  52.3 17.7 %collective-permute-start.5 = (f32[4]{0:T(128)S(1)}, f32[4]{0:T(128)S(1)}, u32[]{:S(2)}, u32[]{:S(2)}) collective-permute-start(f32[4]{0:T(128)S(1)} %get-tuple-element.40), channel_id=1, source_target_pairs={{0,48},{16,64},{32,80},{48,96},{64,112},{80,128},{96,144},{112,160... | collective-permute-start | bytes 56 | tf_op jit(solution)/shard_map/ppermute | solution.py:46
  59.4 14.2 %collective-permute-start.3 = (f32[4]{0:T(128)S(1)}, f32[4]{0:T(128)S(1)}, u32[]{:S(2)}, u32[]{:S(2)}) collective-permute-start(f32[4]{0:T(128)S(1)} %get-tuple-element.40), channel_id=1, source_target_pairs={{0,32},{16,48},{32,64},{48,80},{64,96},{80,112},{96,128},{112,144}... | collective-permute-start | bytes 56 | tf_op jit(solution)/shard_map/ppermute | solution.py:46
  70.0 4.9 %collective-permute-start.1 = (f32[4]{0:T(128)S(1)}, f32[4]{0:T(128)S(1)}, u32[]{:S(2)}, u32[]{:S(2)}) collective-permute-start(f32[4]{0:T(128)S(1)} %get-tuple-element.40), channel_id=1, source_target_pairs={{0,16},{16,32},{32,48},{48,64},{64,80},{80,96},{96,112},{112,128},... | collective-permute-start | bytes 56 | tf_op jit(solution)/shard_map/ppermute | solution.py:46
  75.9 43.5 %copy-start.12 = (f32[4,128,128]{2,1,0:T(8,128)S(1)}, f32[4,128,128]{2,1,0:T(8,128)}, u32[]{:S(2)}) copy-start(f32[4,128,128]{2,1,0:T(8,128)} %get-tuple-element.58) | copy-start | bytes 786436
  75.9 42.8 %collective-permute-start.10 = (f32[4,128,128]{2,1,0:T(8,128)}, f32[4,128,128]{2,1,0:T(8,128)S(1)}, u32[]{:S(2)}, u32[]{:S(2)}) collective-permute-start(f32[4,128,128]{2,1,0:T(8,128)} %get-tuple-element.57), channel_id=1, source_target_pairs={{0,192},{16,208},{32,224},{48,240},{1,193},{17,209},{33,225},{49,2... | collective-permute-start | bytes 786440 | tf_op jit(solution)/shard_map/ppermute | solution.py:46
  93.2 25.5 %collective-permute-start.8 = (f32[4,128,128]{2,1,0:T(8,128)}, f32[4,128,128]{2,1,0:T(8,128)}, u32[]{:S(2)}, u32[]{:S(2)}) collective-permute-start(f32[4,128,128]{2,1,0:T(8,128)} %get-tuple-element.57), channel_id=1, source_target_pairs={{0,128},{16,144},{32,160},{48,176},{64,192},{80,208},{96,224},{112... | collective-permute-start | bytes 786440 | tf_op jit(solution)/shard_map/ppermute | solution.py:46
  95.2 23.5 %collective-permute-start.6 = (f32[4,128,128]{2,1,0:T(8,128)}, f32[4,128,128]{2,1,0:T(8,128)}, u32[]{:S(2)}, u32[]{:S(2)}) collective-permute-start(f32[4,128,128]{2,1,0:T(8,128)} %get-tuple-element.57), channel_id=1, source_target_pairs={{0,64},{16,80},{32,96},{48,112},{64,128},{80,144},{96,160},{112,17... | collective-permute-start | bytes 786440 | tf_op jit(solution)/shard_map/ppermute | solution.py:46
  99.1 9.5 %collective-permute-start.9 = (f32[4]{0:T(128)S(1)}, f32[4]{0:T(128)S(1)}, u32[]{:S(2)}, u32[]{:S(2)}) collective-permute-start(f32[4]{0:T(128)S(1)} %get-tuple-element.66), channel_id=1, source_target_pairs={{0,128},{16,144},{32,160},{48,176},{64,192},{80,208},{96,224},{112... | collective-permute-start | bytes 56 | tf_op jit(solution)/shard_map/ppermute | solution.py:46
  100.4 18.2 %collective-permute-start.7 = (f32[4]{0:T(128)S(1)}, f32[4]{0:T(128)S(1)}, u32[]{:S(2)}, u32[]{:S(2)}) collective-permute-start(f32[4]{0:T(128)S(1)} %get-tuple-element.66), channel_id=1, source_target_pairs={{0,64},{16,80},{32,96},{48,112},{64,128},{80,144},{96,160},{112,17... | collective-permute-start | bytes 56 | tf_op jit(solution)/shard_map/ppermute | solution.py:46
  167.6 141.6 %reduce-scatter.7.cloned.1.call-start = ((), (), s32[]{:S(2)}) async-start(), calls=%async_computation.5 | async-start | bytes 655360
  172.1 5.5 %collective-permute-start.23 = (f32[4]{0:T(128)S(1)}, f32[4]{0:T(128)S(1)}, u32[]{:S(2)}, u32[]{:S(2)}) collective-permute-start(f32[4]{0:T(128)S(1)} %get-tuple-element.43), channel_id=1, source_target_pairs={{128,0},{144,16},{160,32},{176,48},{192,64},{208,80},{224,96},{240... | collective-permute-start | bytes 56 | tf_op jit(solution)/shard_map/ppermute | solution.py:46
  173.4 9.4 %collective-permute-start.21 = (f32[4]{0:T(128)S(1)}, f32[4]{0:T(128)S(1)}, u32[]{:S(2)}, u32[]{:S(2)}) collective-permute-start(f32[4]{0:T(128)S(1)} %get-tuple-element.43), channel_id=1, source_target_pairs={{64,0},{80,16},{96,32},{112,48},{128,64},{144,80},{160,96},{176,11... | collective-permute-start | bytes 56 | tf_op jit(solution)/shard_map/ppermute | solution.py:46
  183.2 28.3 %collective-permute-start.18 = (f32[4,128,128]{2,1,0:T(8,128)S(1)}, f32[4,128,128]{2,1,0:T(8,128)S(1)}, u32[]{:S(2)}, u32[]{:S(2)}) collective-permute-start(f32[4,128,128]{2,1,0:T(8,128)S(1)} %fusion.32), channel_id=1, source_target_pairs={{48,0},{64,16},{80,32},{96,48},{112,64},{128,80},{144,96},{160,112... | collective-permute-start | bytes 786440 | tf_op jit(solution)/shard_map/ppermute | solution.py:46
  184.6 26.9 %collective-permute-start.16 = (f32[4,128,128]{2,1,0:T(8,128)S(1)}, f32[4,128,128]{2,1,0:T(8,128)S(1)}, u32[]{:S(2)}, u32[]{:S(2)}) collective-permute-start(f32[4,128,128]{2,1,0:T(8,128)S(1)} %fusion.32), channel_id=1, source_target_pairs={{32,0},{48,16},{64,32},{80,48},{96,64},{112,80},{128,96},{144,112}... | collective-permute-start | bytes 786440 | tf_op jit(solution)/shard_map/ppermute | solution.py:46
  185.9 25.6 %collective-permute-start.14 = (f32[4,128,128]{2,1,0:T(8,128)S(1)}, f32[4,128,128]{2,1,0:T(8,128)S(1)}, u32[]{:S(2)}, u32[]{:S(2)}) collective-permute-start(f32[4,128,128]{2,1,0:T(8,128)S(1)} %fusion.32), channel_id=1, source_target_pairs={{16,0},{32,16},{48,32},{64,48},{80,64},{96,80},{112,96},{128,112},... | collective-permute-start | bytes 786440 | tf_op jit(solution)/shard_map/ppermute | solution.py:46
  212.4 72.0 %collective-permute-start.24 = (f32[4,128,128]{2,1,0:T(8,128)}, f32[4,128,128]{2,1,0:T(8,128)}, u32[]{:S(2)}, u32[]{:S(2)}) collective-permute-start(f32[4,128,128]{2,1,0:T(8,128)} %get-tuple-element.47), channel_id=1, source_target_pairs={{192,0},{208,16},{224,32},{240,48},{193,1},{209,17},{225,33},{241,... | collective-permute-start | bytes 786440 | tf_op jit(solution)/shard_map/ppermute | solution.py:46
  213.6 70.7 %collective-permute-start.22 = (f32[4,128,128]{2,1,0:T(8,128)}, f32[4,128,128]{2,1,0:T(8,128)}, u32[]{:S(2)}, u32[]{:S(2)}) collective-permute-start(f32[4,128,128]{2,1,0:T(8,128)} %get-tuple-element.47), channel_id=1, source_target_pairs={{128,0},{144,16},{160,32},{176,48},{192,64},{208,80},{224,96},{240... | collective-permute-start | bytes 786440 | tf_op jit(solution)/shard_map/ppermute | solution.py:46
  214.9 69.4 %collective-permute-start.20 = (f32[4,128,128]{2,1,0:T(8,128)}, f32[4,128,128]{2,1,0:T(8,128)}, u32[]{:S(2)}, u32[]{:S(2)}) collective-permute-start(f32[4,128,128]{2,1,0:T(8,128)} %get-tuple-element.47), channel_id=1, source_target_pairs={{64,0},{80,16},{96,32},{112,48},{128,64},{144,80},{160,96},{176,11... | collective-permute-start | bytes 786440 | tf_op jit(solution)/shard_map/ppermute | solution.py:46
  (26 other events, 361.5 us)
Sparse Core Ops, SparseCore 0:
  9.8 44.8 all-gather.4
  56.5 92.5 all-gather.2
  167.7 114.5 reduce-scatter.4
  284.7 24.4 reduce-scatter.6
